TPU v7x, 32 devices: a whole 2x2x4 slice. The times are simulated.
32 devices in a mesh: ctx: 8 (over y, x, core), dp: 4 (over z).
Axes of the slice: x: 2, y: 2, z: 4, core: 2. Of those that a mesh axis runs over, the one named last changes fastest.
Arguments:
- tokens: bfloat16 [4, 1024, 4096], P('dp', 'ctx'), may hold values from -64 to 64
- query_weight: bfloat16 [4096, 4096], P('dp', 'ctx'), may hold values from -0.09375 to 0.09375
- keyval_matrix: bfloat16 [4096, 1024], P('dp', 'ctx'), may hold values from -0.09375 to 0.09375
- grad_out: bfloat16 [4, 1024, 4096], P('dp', 'ctx'), may hold values from -6 to 6
- blocks: int32 [4, 8, 8], replicated, may hold values from 0 to 7, as said below
- counts: int32 [4, 8], replicated, may hold values from 4 to 8, as said below
Outputs:
- attended: bfloat16 [4, 1024, 4096], P('dp', 'ctx')
- grad_query_weight: float32 [4096, 4096], P('dp', 'ctx')
- grad_keyval_weight: float32 [4096, 1024], P('dp', 'ctx')
Inputs may be any that keep to these rules, and one draw needn't show every extreme that they name: For key head g and query block i, the first counts[g, i] entries of blocks[g, i] are distinct; they are the blocks i - 1, i, i + 1, 0 and 7 that exist, then random others. Entries from counts[g, i] on are block numbers that are not attended. counts[g, i] is the number of distinct blocks among i - 1, i, i + 1, 0 and 7 that exist, plus 1 to 3.
All inputs are finite; a program needn't handle non-finite values.
Results may differ from a plain program's by a relative error of at most 0.004.
The roundings to bfloat16 on the way count: a program that leaves them out, or rounds other values in their place, can miss the bound.
Values may be sent and summed in bfloat16 or wider, within the bound.
No kernel may reach another device: no remote copies, remote signals or barrier semaphores. Data moves between devices by JAX's collectives and lax.ppermute only.
A program may use at most 128 MiB of HBM per device.

v0:
```python
import jax
import jax.numpy as jnp
from jax import lax
from jax.sharding import PartitionSpec as P


def partner(block, axis, distance):
    count = lax.axis_size(axis)
    route = []
    for low in range(count):
        high = low | 1 << distance
        if high != low and high < count:
            route += [(low, high), (high, low)]
    return lax.ppermute(block, axis, route)


def attend_part(query_rows, key_rows, vals, dout, valid, scale):
    scores = (
        jnp.einsum("nqhd,nkcd->nhqkc", query_rows, key_rows, preferred_element_type=jnp.float32)
        * scale
    )
    scores = jnp.where(valid[:, None, None, :, None], scores, -jnp.inf)
    peak = jnp.max(scores, axis=(3, 4), keepdims=True)
    expo = jnp.exp(scores - peak)
    probs = expo / jnp.sum(expo, axis=(3, 4), keepdims=True)
    probs_b = probs.astype(jnp.bfloat16)
    out = jnp.einsum("nhqkc,nkcd->nqhd", probs_b, vals, preferred_element_type=jnp.float32).astype(
        jnp.bfloat16
    )
    delta = jnp.transpose(
        jnp.sum(dout.astype(jnp.float32) * out.astype(jnp.float32), axis=3), (0, 2, 1)
    )
    dprob = jnp.einsum("nqhd,nkcd->nhqkc", dout, vals, preferred_element_type=jnp.float32)
    dscore = (probs * (dprob - delta[:, :, :, None, None]) * scale).astype(jnp.bfloat16)
    dquery = jnp.einsum(
        "nhqkc,nkcd->nqhd", dscore, key_rows, preferred_element_type=jnp.float32
    ).astype(jnp.bfloat16)
    dkeys = jnp.einsum("nhqkc,nqhd->nkcd", dscore, query_rows, preferred_element_type=jnp.float32)
    dvals = jnp.einsum("nhqkc,nqhd->nkcd", probs_b, dout, preferred_element_type=jnp.float32)
    return (out, dquery, dkeys, dvals)


def attention(q_heads, keyval_rows, dout_heads, blk, cnt):
    length = q_heads.shape[0]
    head_size = keyval_rows.shape[1] // 2
    heads = q_heads.shape[1] // head_size
    nblocks, kslots = blk.shape
    block = length // nblocks
    scale = head_size ** (-0.5)
    step = 4
    groups = nblocks // step
    key_rows = keyval_rows[:, :head_size].reshape(nblocks, block, head_size)
    vals = keyval_rows[:, head_size:].reshape(nblocks, block, head_size)
    valid = lax.broadcasted_iota(jnp.int32, (nblocks, kslots), 1) < cnt[:, None]
    query_rows = q_heads.reshape(groups, step, block, heads, head_size)
    dout = dout_heads.reshape(groups, step, block, heads, head_size)

    def one_step(args):
        q_part, d_part, b_part, v_part = args
        return attend_part(q_part, key_rows[b_part], vals[b_part], d_part, v_part, scale)

    out, dquery, dkeys, dvals = lax.map(
        one_step,
        (query_rows, dout, blk.reshape(groups, step, kslots), valid.reshape(groups, step, kslots)),
    )
    dkeys = dkeys.reshape(nblocks, kslots, block, head_size)
    dvals = dvals.reshape(nblocks, kslots, block, head_size)
    onehot = (
        (blk[None, :, :] == lax.broadcasted_iota(jnp.int32, (nblocks, 1, 1), 0)) & valid[None]
    ).astype(jnp.float32)
    key_grad = jnp.einsum("bnk,nkcd->bcd", onehot, dkeys, precision=lax.Precision.HIGHEST)
    val_grad = jnp.einsum("bnk,nkcd->bcd", onehot, dvals, precision=lax.Precision.HIGHEST)
    keyval_grad = jnp.concatenate(
        [key_grad.reshape(length, head_size), val_grad.reshape(length, head_size)], axis=1
    )
    return (
        out.reshape(length, heads * head_size),
        dquery.reshape(length, heads * head_size),
        keyval_grad,
    )


def shards(tokens, query_weight, keyval_matrix, grad_out, blocks, counts):
    local_rows = tokens[0]
    group_size = lax.axis_size("ctx") // blocks.shape[0]
    group_bits = group_size.bit_length() - 1
    device = lax.axis_index("ctx")
    query_cols = query_weight.shape[1]
    weights_full = lax.all_gather(
        jnp.concatenate([query_weight, keyval_matrix], axis=1), "dp", axis=0, tiled=True
    )
    query_full = weights_full[:, :query_cols]
    keyval_part = weights_full[:, query_cols:]
    all_rows = lax.all_gather(local_rows, "ctx", axis=0, tiled=True)
    keyval_cols = keyval_part
    for bit in range(group_bits):
        other = partner(keyval_cols, "ctx", bit)
        upper = device >> bit & 1 == 1
        keyval_cols = jnp.where(
            upper,
            jnp.concatenate([other, keyval_cols], axis=1),
            jnp.concatenate([keyval_cols, other], axis=1),
        )
    projected = jnp.dot(
        all_rows,
        jnp.concatenate([query_full, keyval_cols], axis=1),
        preferred_element_type=jnp.float32,
    ).astype(jnp.bfloat16)
    q_heads = projected[:, :query_cols]
    keyval_rows = projected[:, query_cols:]
    dout_heads = lax.all_to_all(grad_out[0], "ctx", split_axis=1, concat_axis=0, tiled=True)
    group_index = device // group_size
    blk = lax.dynamic_index_in_dim(blocks, group_index, 0, keepdims=False)
    cnt = lax.dynamic_index_in_dim(counts, group_index, 0, keepdims=False)
    out_heads, dquery, keyval_grad = attention(q_heads, keyval_rows, dout_heads, blk, cnt)
    attended = lax.all_to_all(out_heads, "ctx", split_axis=0, concat_axis=1, tiled=True)
    summed = keyval_grad
    for bit in range(group_bits):
        summed = summed + partner(summed, "ctx", bit)
    width = summed.shape[1] // group_size
    own_grad = lax.dynamic_slice_in_dim(summed, device % group_size * width, width, 1)
    own_grad = own_grad.astype(jnp.bfloat16)
    contract = (((0,), (0,)), ((), ()))
    grad_query = lax.dot_general(all_rows, dquery, contract, preferred_element_type=jnp.float32)
    grad_keyval = lax.dot_general(all_rows, own_grad, contract, preferred_element_type=jnp.float32)
    grads = lax.psum_scatter(
        jnp.concatenate([grad_query, grad_keyval], axis=1), "dp", scatter_dimension=0, tiled=True
    )
    grad_query = grads[:, :query_cols]
    grad_keyval = grads[:, query_cols:]
    return (attended[None], grad_query, grad_keyval)


def solution(mesh):
    in_specs = (
        P("dp", "ctx", None),
        P("dp", "ctx"),
        P("dp", "ctx"),
        P("dp", "ctx", None),
        P(),
        P(),
    )
    out_specs = (P("dp", "ctx", None), P("dp", "ctx"), P("dp", "ctx"))
    return jax.shard_map(shards, mesh=mesh, in_specs=in_specs, out_specs=out_specs, check_vma=False)
```

profile of v0, /device:TPU:0, one launch (start us, length us, event | category | flops | bytes accessed | tf_op | source)
XLA Modules:
  0.0 476.8 jit_solution(18149583840988707000)
XLA Ops:
  7.2 2.6 pad_maximum_fusion.1
  10.6 100.4 %all-gather.4.cloned.1.call-done = bf16[4096,640]{1,0:T(8,128)(2,1)} async-done(((bf16[1024,640]{1,0:T(8,128)(2,1)}), bf16[4096,640]{1,0:T(8,128)(2,1)}) %all-gather.4.cloned.1.call-update) | async-done | bytes 5242896 | tf_op jit(solution)/shard_map/all_gather | solution.py:89
  113.6 4.2 all-to-all-start
  120.1 4.6 slice.35
  124.7 2.1 maximum_select_fusion
  126.9 46.3 %all-gather.6.cloned.1.call-done = bf16[1,1024,4096]{2,1,0:T(8,128)(2,1)} async-done(((bf16[1,128,4096]{2,1,0:T(8,128)(2,1)}), bf16[1,1024,4096]{2,1,0:T(8,128)(2,1)}) %all-gather.6.cloned.1.call-update) | async-done | bytes 8388624 | tf_op jit(solution)/shard_map/all_gather | solution.py:94
  173.1 10.4 %fusion.56 = bf16[1024,768]{0,1:T(8,128)(2,1)S(1)} fusion(bf16[1,1024,4096]{2,1,0:T(8,128)(2,1)} %all-gather.6.cloned.1.call-done, bf16[4096,256]{1,0:T(8,128)(2,1)S(1)} %maximum_select_fusion, bf16[4096,512]{1,0:T(8,128)(2,1)} %slice.35), kind=kOutput, calls=%fused_computation.58 | convolution fusion | flops 6455820288 | bytes 16252928 | tf_op jit(solution)/shard_map/dot_general | solution.py:104
  185.6 65.5 %while.16 = (s32[]{:T(128)}, bf16[2,4,128,4,128]{2,4,3,1,0:T(8,128)(2,1)}, bf16[2,4,128,4,128]{4,3,2,1,0:T(4,128)(2,1)}, f32[2,4,8,128,128]{4,3,2,1,0:T(8,128)},...) while((s32[]{:T(128)}, ...), condition=%wide.region_4.5_spmd, body=%wide.region_0.4_spmd.sunk | while | flops 3275222016 | bytes 218726320 | solution.py:62
  191.4 3.4 copy-done.6
  194.8 3.2 bitcast_dynamic-update-slice_fusion.8
  200.7 6.5 %bitcast_dynamic-update-slice_fusion.6 = (bf16[2,4,128,4,128]{2,4,3,1,0:T(8,128)(2,1)}, bf16[4,128,4,128]{3,1,2,0:T(8,128)(2,1)S(1)}) fusion(bf16[2,4,128,4,128]{2,4,3,1,0:T(8,128)(2,1)} %get-tuple-element.241, s32[]{:T(128)} %get-tuple-element.240, bf16[4,8,128,128,1]{3,2,4,1,0:T(8,128)(2,1)S(1)} %bitcast.231, f32[4,4,128]{2,1,0:T(4,128)S(1)} %fusion.119, ...), kind=kOutput, calls=%fused_computation.26.clone.1 | convolution fusion | flops 547618816 | bytes 10502688 | tf_op jit(solution)/shard_map/while/body/eval_jaxpr/nhqkc,nkcd->nqhd/dot_general | solution.py:27
  208.5 4.3 fusion.120
  214.1 2.0 copy-done.5
  224.0 3.4 copy-done.6
  227.4 3.2 bitcast_dynamic-update-slice_fusion.8
  233.3 6.5 %bitcast_dynamic-update-slice_fusion.6 = (bf16[2,4,128,4,128]{2,4,3,1,0:T(8,128)(2,1)}, bf16[4,128,4,128]{3,1,2,0:T(8,128)(2,1)S(1)}) fusion(bf16[2,4,128,4,128]{2,4,3,1,0:T(8,128)(2,1)} %get-tuple-element.241, s32[]{:T(128)} %get-tuple-element.240, bf16[4,8,128,128,1]{3,2,4,1,0:T(8,128)(2,1)S(1)} %bitcast.231, f32[4,4,128]{2,1,0:T(4,128)S(1)} %fusion.119, ...), kind=kOutput, calls=%fused_computation.26.clone.1 | convolution fusion | flops 547618816 | bytes 10502688 | tf_op jit(solution)/shard_map/while/body/eval_jaxpr/nhqkc,nkcd->nqhd/dot_general | solution.py:27
  241.1 4.3 fusion.120
  251.1 7.2 %fusion.61 = f32[8,128,128]{2,0,1:T(8,128)S(1)} fusion(f32[8,8,128,128]{3,2,1,0:T(8,128)} %bitcast.237, s32[8,8]{0,1:T(8,128)S(1)} %copy-done.14, pred[8,8]{0,1:T(8,128)(4,1)S(1)} %copy-done.15), kind=kOutput, calls=%fused_computation.63 | convolution fusion | flops 100664320 | bytes 4718912 | tf_op jit(solution)/shard_map/bnk,nkcd->bcd/dot_general | solution.py:71
  258.4 5.0 %fusion.64 = f32[8,128,128]{2,0,1:T(8,128)S(1)} fusion(f32[8,8,128,128]{3,2,1,0:T(8,128)S(1)} %bitcast.238, s32[8,8]{0,1:T(8,128)S(1)} %copy-done.14, pred[8,8]{0,1:T(8,128)(4,1)S(1)} %copy-done.15), kind=kOutput, calls=%fused_computation.64 | convolution fusion | flops 100664320 | bytes 4718912 | tf_op jit(solution)/shard_map/bnk,nkcd->bcd/dot_general | solution.py:72
  263.9 10.2 %fusion.38 = f32[4096,512]{0,1:T(8,128)} fusion(bf16[1,1024,4096]{2,1,0:T(8,128)(2,1)} %all-gather.6.cloned.1.call-done, bf16[128,8,4,128]{3,2,1,0:T(4,128)(2,1)S(1)} %bitcast.240), kind=kOutput, calls=%fused_computation.47 | convolution fusion | flops 4294967296 | bytes 17825792 | tf_op jit(solution)/shard_map/dot_general | solution.py:124
  274.1 4.9 %fusion.44 = f32[4096,128]{0,1:T(8,128)S(1)} fusion(bf16[1,1024,4096]{2,1,0:T(8,128)(2,1)} %all-gather.6.cloned.1.call-done, s32[]{:T(128)S(6)} %select_n.51, f32[1024,128]{1,0:T(8,128)S(1)} %bitcast.234, f32[1024,128]{1,0:T(8,128)S(1)} %bitcast.236, f32[1024,256]{1,0:T(8,128)} %collective-permute-done.1), kind=kOutput, calls=%fused_computation.51 | convolution fusion | flops 1074135040 | bytes 12058628 | tf_op jit(solution)/shard_map/dot_general | solution.py:125
  279.0 8.6 %pad_maximum_fusion = f32[4096,640]{0,1:T(8,128)} fusion(f32[4096,128]{0,1:T(8,128)S(1)} %fusion.44, f32[4096,512]{0,1:T(8,128)} %fusion.38), kind=kLoop, calls=%fused_computation.40 | loop fusion | flops 2621440 | bytes 20971520 | tf_op jit(solution)/shard_map/concatenate | solution.py:127
  289.4 17.9 %all_to_all.32 = bf16[8,128,512]{2,1,0:T(8,128)(2,1)S(1)} all-to-all(bf16[8,128,512]{2,1,0:T(8,128)(2,1)S(1)} %copy.112), channel_id=1, replica_groups=mesh['ctx'=8,'dp'=4] {'ctx'}, dimensions={0} | all-to-all | bytes 2097152 | tf_op jit(solution)/shard_map/all_to_all | solution.py:116
  309.3 156.5 %reduce-scatter.2.cloned.1.call-done = f32[1024,640]{0,1:T(8,128)} async-done(((f32[4096,640]{0,1:T(8,128)}), f32[1024,640]{0,1:T(8,128)}) %reduce-scatter.2.cloned.1.call-update) | async-done | bytes 2621456 | tf_op jit(solution)/shard_map/reduce_scatter | solution.py:126
  (116 shorter events, 44.5 us)
Async XLA Ops:
  7.2 111.6 %copy-start = (s32[4,8,8]{2,1,0:T(8,128)S(1)}, s32[4,8,8]{2,1,0:T(8,128)}, u32[]{:S(2)}) copy-start(s32[4,8,8]{2,1,0:T(8,128)} %param.12) | copy-start | bytes 3076
  7.2 105.2 %copy-start.12 = (bf16[1,128,4096]{2,1,0:T(8,128)(2,1)S(1)}, bf16[1,128,4096]{2,1,0:T(8,128)(2,1)}, u32[]{:S(2)}) copy-start(bf16[1,128,4096]{2,1,0:T(8,128)(2,1)} %param.11) | copy-start | bytes 3145732
  7.2 103.8 %all-gather.4.cloned.1.call-start = ((), (), s32[]{:S(2)}) async-start(), calls=%async_computation.3 | async-start | bytes 6553600 | tf_op jit(solution)/shard_map/all_gather | solution.py:89
  9.8 163.3 %all-gather.6.cloned.1.call-start = ((), (), s32[]{:S(2)}) async-start(), calls=%async_computation.5 | async-start | bytes 9437184 | tf_op jit(solution)/shard_map/all_gather | solution.py:94
  112.3 12.5 %collective-permute-start = (bf16[4096,128]{1,0:T(8,128)(2,1)S(1)}, bf16[4096,128]{1,0:T(8,128)(2,1)}, u32[]{:S(2)}, u32[]{:S(2)}) collective-permute-start(bf16[4096,128]{1,0:T(8,128)(2,1)S(1)} %slice.36), channel_id=1, source_target_pairs={{0,4},{4,0},{8,12},{12,8},{16,20},{20,16},{24,28},{28,24},{1,5},{5... | collective-permute-start | bytes 3145736 | tf_op jit(solution)/shard_map/ppermute | solution.py:14
  113.6 71.9 %all-to-all-start = ((bf16[128,8,512]{0,2,1:T(8,128)(2,1)}), bf16[128,8,512]{0,2,1:T(8,128)(2,1)}, u32[]{:S(2)}, u32[]{:S(2)}) async-start(bf16[128,8,512]{0,2,1:T(8,128)(2,1)} %bitcast.39), calls=%async_computation | async-start | bytes 2097152 | tf_op jit(solution)/shard_map/all_to_all | solution.py:111
  117.9 347.9 %reduce-scatter.2.cloned.1.call-start = ((), (), s32[]{:S(2)}) async-start(), calls=%async_computation.4 | async-start | bytes 13107200 | tf_op jit(solution)/shard_map/reduce_scatter | solution.py:126
  185.6 65.5 %copy-start.14 = (s32[8,8]{0,1:T(8,128)S(1)}, s32[8,8]{0,1:T(8,128)}, u32[]{:S(2)}) copy-start(s32[8,8]{0,1:T(8,128)} %copy.76) | copy-start | bytes 772
  185.6 65.5 %copy-start.15 = (pred[8,8]{0,1:T(8,128)(4,1)S(1)}, pred[8,8]{0,1:T(8,128)(4,1)}, u32[]{:S(2)}) copy-start(pred[8,8]{0,1:T(8,128)(4,1)} %iota_compare_fusion.1) | copy-start | bytes 196
  189.5 8.4 %copy-start.2 = (f32[4,8,128,128,4]{3,2,4,1,0:T(8,128)}, f32[4,8,128,128,4]{3,2,4,1,0:T(8,128)S(1)}, u32[]{:S(2)}) copy-start(f32[4,8,128,128,4]{3,2,4,1,0:T(8,128)S(1)} %get-tuple-element.224) | copy-start | bytes 25165828 | tf_op jit(solution)/shard_map/while
  189.6 5.2 %copy-start.6 = (f32[2,4,8,128,128]{4,3,2,1,0:T(8,128)S(1)}, f32[2,4,8,128,128]{4,3,2,1,0:T(8,128)}, u32[]{:S(2)}) copy-start(f32[2,4,8,128,128]{4,3,2,1,0:T(8,128)} %get-tuple-element.244) | copy-start | bytes 12582916 | tf_op jit(solution)/shard_map/while
  200.7 7.8 %copy-start.3 = (f32[4,8,128,128,4]{3,2,4,1,0:T(8,128)S(1)}, f32[4,8,128,128,4]{3,2,4,1,0:T(8,128)}, u32[]{:S(2)}) copy-start(f32[4,8,128,128,4]{3,2,4,1,0:T(8,128)} %copy-done.2) | copy-start | bytes 25165828 | tf_op jit(solution)/shard_map/while
  208.4 4.4 copy-start.4
  212.8 4.4 copy-start.9
  222.2 8.4 %copy-start.2 = (f32[4,8,128,128,4]{3,2,4,1,0:T(8,128)}, f32[4,8,128,128,4]{3,2,4,1,0:T(8,128)S(1)}, u32[]{:S(2)}) copy-start(f32[4,8,128,128,4]{3,2,4,1,0:T(8,128)S(1)} %get-tuple-element.224) | copy-start | bytes 25165828 | tf_op jit(solution)/shard_map/while
  222.2 5.2 %copy-start.6 = (f32[2,4,8,128,128]{4,3,2,1,0:T(8,128)S(1)}, f32[2,4,8,128,128]{4,3,2,1,0:T(8,128)}, u32[]{:S(2)}) copy-start(f32[2,4,8,128,128]{4,3,2,1,0:T(8,128)} %get-tuple-element.244) | copy-start | bytes 12582916 | tf_op jit(solution)/shard_map/while
  233.3 7.8 %copy-start.3 = (f32[4,8,128,128,4]{3,2,4,1,0:T(8,128)S(1)}, f32[4,8,128,128,4]{3,2,4,1,0:T(8,128)}, u32[]{:S(2)}) copy-start(f32[4,8,128,128,4]{3,2,4,1,0:T(8,128)} %copy-done.2) | copy-start | bytes 25165828 | tf_op jit(solution)/shard_map/while
  241.1 4.4 copy-start.4
  245.4 4.4 copy-start.9
  251.1 7.4 %copy-start.8 = (f32[2,4,8,128,128]{4,3,2,1,0:T(8,128)S(1)}, f32[2,4,8,128,128]{4,3,2,1,0:T(8,128)}, u32[]{:S(2)}) copy-start(f32[2,4,8,128,128]{4,3,2,1,0:T(8,128)} %get-tuple-element.66) | copy-start | bytes 12582916
  258.3 5.6 %copy-start.11 = (bf16[2,4,128,4,128]{4,3,2,1,0:T(4,128)(2,1)S(1)}, bf16[2,4,128,4,128]{4,3,2,1,0:T(4,128)(2,1)}, u32[]{:S(2)}) copy-start(bf16[2,4,128,4,128]{4,3,2,1,0:T(4,128)(2,1)} %get-tuple-element.64) | copy-start | bytes 3145732
  263.6 10.5 %collective-permute-start.1 = (f32[1024,256]{1,0:T(8,128)S(1)}, f32[1024,256]{1,0:T(8,128)}, u32[]{:S(2)}, u32[]{:S(2)}) collective-permute-start(f32[1024,256]{1,0:T(8,128)S(1)} %pad_maximum_fusion.2), channel_id=1, source_target_pairs={{0,4},{4,0},{8,12},{12,8},{16,20},{20,16},{24,28},{28,24},{1,5},{5... | collective-permute-start | bytes 3145736 | tf_op jit(solution)/shard_map/ppermute | solution.py:14
  308.0 162.3 %copy-start.1 = (s32[4,8,8]{2,1,0:T(8,128)S(1)}, s32[4,8,8]{2,1,0:T(8,128)}, u32[]{:S(2)}) copy-start(s32[4,8,8]{2,1,0:T(8,128)} %param.12) | copy-start | bytes 3076
  465.8 3.4 slice-start.1
  (8 other events, 12.6 us)
Sparse Core Ops, SparseCore 0:
  10.2 100.7 all-gather.3
  112.8 60.2 all-gather.5
  287.8 178.0 reduce-scatter.1
where the time goes:
time: 478 us; the launch traced here: 477 us
  waiting for transfers between devices  304 us (64%)
  matrix products  72.5 us (15%)
  local copies, waits for them, and re-layouts  43 us (9%)
  other arithmetic  20.1 us (4%)
  blocking collectives  17.9 us (4%)
  between operations  14 us (3%)
    reduce_scatter x1, waiting for transfers between devices, shards(): lax.psum_scatter(jnp.concatenate([grad_query, grad_keyval], axis=1), 'dp'...  157 us
    all_gather x1, waiting for transfers between devices, shards(): lax.all_gather(jnp.concatenate([query_weight, keyval_matrix], axis=1), 'd...  100 us
    all_gather x1, waiting for transfers between devices, shards(): all_rows = lax.all_gather(local_rows, 'ctx', axis=0, tiled=True)  46.3 us
    all_to_all x1, blocking collectives, shards(): lax.all_to_all(out_heads, 'ctx', split_axis=0, concat_axis=1, tiled=True)  17.9 us
    while x32, local copies, waits for them, and re-layouts  16.5 us
    dot_general x2, matrix products, attend_part(): jnp.einsum('nhqkc,nkcd->nqhd', probs_b, vals, preferred_element_type=jnp....  13.1 us
    dot_general x1, matrix products, shards(): jnp.dot(all_rows, jnp.concatenate([query_full, keyval_cols], axis=1), pre...  10.4 us
    dot_general x1, matrix products, shards(): lax.dot_general(all_rows, dquery, contract, preferred_element_type=jnp.fl...  10.2 us
  transfers between devices with their start and end apart: 6, of which 3 were waited for; matrix products, arithmetic and copies ran while one was open for 8% of the time, Pallas kernels for 0%

commit v1 on v0

--- a/solution.py
+++ b/solution.py
@@ -91,7 +91,25 @@
     )
     query_full = weights_full[:, :query_cols]
     keyval_part = weights_full[:, query_cols:]
-    all_rows = lax.all_gather(local_rows, "ctx", axis=0, tiled=True)
+    local_out = lax.psum(1, axis_name="ctx")
+    mid_arr = lax.axis_index("ctx")
+    prior, base_arr, local_now = (local_out, mid_arr, local_rows.shape[0])
+    items = tuple((m * prior if h == 0 else m for h, m in enumerate(local_rows.shape)))
+    arr_next = jnp.zeros(items, local_rows.dtype)
+    u1 = after = local_rows
+    all_rows = lax.dynamic_update_slice_in_dim(arr_next, local_rows, base_arr * local_now, axis=0)
+    for jj in range(1, prior // 2 + 1):
+        w1 = tuple(((h, (h + 1) % prior) for h in range(prior)))
+        u1 = lax.ppermute(u1, axis_name="ctx", perm=w1)
+        all_rows = lax.dynamic_update_slice_in_dim(
+            all_rows, u1, (base_arr - jj) % prior * local_now, axis=0
+        )
+        if 2 * jj < prior:
+            long_array = tuple(((h, (h - 1) % prior) for h in range(prior)))
+            after = lax.ppermute(after, axis_name="ctx", perm=long_array)
+            all_rows = lax.dynamic_update_slice_in_dim(
+                all_rows, after, (base_arr + jj) % prior * local_now, axis=0
+            )
     keyval_cols = keyval_part
     for bit in range(group_bits):
         other = partner(keyval_cols, "ctx", bit)

time: 478 us -> 413 us (0.86)
  waiting for transfers between devices: 304 us -> 225 us
  starting transfers between devices: 4.76 us -> 15.1 us
  local copies, waits for them, and re-layouts: 43 us -> 50.5 us
    all_gather x1, waiting for transfers between devices: 100 us -> 19.4 us  [shards(): lax.all_gather(jnp.concatenate([query_weight, keyval_matrix], axis=1), 'd...]
    ppermute x0 -> x7, waiting for transfers between devices: none -> 51.8 us  [the longest x4 51.8 us: shards(): u1 = lax.ppermute(u1, axis_name='ctx', perm=w1)]
    all_gather x1 -> x0, waiting for transfers between devices: 46.3 us -> none  [shards(): all_rows = lax.all_gather(local_rows, 'ctx', axis=0, tiled=True)]
    dynamic_update_slice x0 -> x8, local copies, waits for them, and re-layouts: none -> 13 us  [the longest x4 8.74 us: shards(): lax.dynamic_update_slice_in_dim(all_rows, u1, (base_arr - jj) % prior * l...]
    ppermute x0 -> x7, starting transfers between devices: none -> 10.7 us  [the longest x3 7.05 us: shards(): after = lax.ppermute(after, axis_name='ctx', perm=long_array)]
    while x34 -> x32, local copies, waits for them, and re-layouts: 16.9 us -> 7.89 us
  transfers between devices with their start and end apart: 6 -> 12, of which waited for: 3 -> 5; matrix products, arithmetic and copies ran while one was open for 8% -> 12% of each run, Pallas kernels for 0% -> 0%
where the time goes in v1:
time: 413 us; the launch traced here: 412 us
  waiting for transfers between devices  225 us (54%)
  matrix products  69.3 us (17%)
  local copies, waits for them, and re-layouts  50.5 us (12%)
  other arithmetic  18.8 us (5%)
  blocking collectives  18.6 us (5%)
  starting transfers between devices  15.1 us (4%)
  between operations  14.4 us (3%)
    reduce_scatter x1, waiting for transfers between devices, shards(): lax.psum_scatter(jnp.concatenate([grad_query, grad_keyval], axis=1), 'dp'...  154 us
    ppermute x4, waiting for transfers between devices, shards(): u1 = lax.ppermute(u1, axis_name='ctx', perm=w1)  51.8 us
    all_gather x1, waiting for transfers between devices, shards(): lax.all_gather(jnp.concatenate([query_weight, keyval_matrix], axis=1), 'd...  19.4 us
    all_to_all x1, blocking collectives, shards(): lax.all_to_all(out_heads, 'ctx', split_axis=0, concat_axis=1, tiled=True)  18.6 us
    dot_general x2, matrix products, attend_part(): jnp.einsum('nhqkc,nkcd->nqhd', probs_b, vals, preferred_element_type=jnp....  13.1 us
    dot_general x1, matrix products, shards(): lax.dot_general(all_rows, dquery, contract, preferred_element_type=jnp.fl...  10.3 us
    dot_general x1, matrix products, shards(): jnp.dot(all_rows, jnp.concatenate([query_full, keyval_cols], axis=1), pre...  9.03 us
    dynamic_update_slice x4, local copies, waits for them, and re-layouts, shards(): lax.dynamic_update_slice_in_dim(all_rows, u1, (base_arr - jj) % prior * l...  8.74 us
  transfers between devices with their start and end apart: 12, of which 5 were waited for; matrix products, arithmetic and copies ran while one was open for 12% of the time, Pallas kernels for 0%

profile of v1, /device:TPU:0, one launch (start us, length us, event | category | flops | bytes accessed | tf_op | source)
XLA Modules:
  0.0 412.5 jit_solution(5609485332407212902)
XLA Ops:
  7.2 2.6 pad_maximum_fusion.1
  10.3 2.9 collective-permute-start.1
  15.6 3.6 all-to-all-start
  21.4 13.2 %collective-permute-done = bf16[128,4096]{1,0:T(8,128)(2,1)} collective-permute-done((bf16[128,4096]{1,0:T(8,128)(2,1)}, bf16[128,4096]{1,0:T(8,128)(2,1)}, u32[]{:S(2)}, u32[]{:S(2)}) %collective-permute-start) | collective-permute-done | bytes 1048608 | tf_op jit(solution)/shard_map/ppermute | solution.py:103
  35.2 4.4 %broadcast_in_dim.43 = bf16[1024,4096]{1,0:T(8,128)(2,1)} broadcast(bf16[]{:T(256)} %constant.106.clone.1), dimensions={} | broadcast | bytes 8388610 | tf_op jit(solution)/shard_map/broadcast_in_dim | solution.py:98
  42.7 25.4 %collective-permute-done.2 = bf16[128,4096]{1,0:T(8,128)(2,1)S(1)} collective-permute-done((bf16[128,4096]{1,0:T(8,128)(2,1)}, bf16[128,4096]{1,0:T(8,128)(2,1)S(1)}, u32[]{:S(2)}, u32[]{:S(2)}) %collective-permute-start.2) | collective-permute-done | bytes 1048608 | tf_op jit(solution)/shard_map/ppermute | solution.py:103
  68.9 2.3 constant_dynamic-update-slice_fusion.7
  75.4 13.2 %collective-permute-done.4 = bf16[128,4096]{1,0:T(8,128)(2,1)} collective-permute-done((bf16[128,4096]{1,0:T(8,128)(2,1)S(1)}, bf16[128,4096]{1,0:T(8,128)(2,1)}, u32[]{:S(2)}, u32[]{:S(2)}) %collective-permute-start.4) | collective-permute-done | bytes 1048608 | tf_op jit(solution)/shard_map/ppermute | solution.py:103
  91.5 19.4 %all-gather.2.cloned.1.call-done = bf16[4096,640]{1,0:T(8,128)(2,1)} async-done(((bf16[1024,640]{1,0:T(8,128)(2,1)}), bf16[4096,640]{1,0:T(8,128)(2,1)}) %all-gather.2.cloned.1.call-update) | async-done | bytes 5242896 | tf_op jit(solution)/shard_map/all_gather | solution.py:89
  112.3 2.4 constant_dynamic-update-slice_fusion.3
  115.8 2.9 constant_dynamic-update-slice_fusion.1
  119.5 9.0 %fusion.38 = bf16[1024,768]{1,0:T(8,128)(2,1)S(1)} fusion(bf16[1024,4096]{1,0:T(8,128)(2,1)} %constant_dynamic-update-slice_fusion.1, bf16[4096,256]{1,0:T(8,128)(2,1)S(1)} %maximum_select_fusion, bf16[4096,512]{1,0:T(8,128)(2,1)S(1)} %slice-done), kind=kOutput, calls=%fused_computation.49 | convolution fusion | flops 6455820288 | bytes 16252928 | tf_op jit(solution)/shard_map/dot_general | solution.py:122
  132.0 55.8 %while.16 = (s32[]{:T(128)}, bf16[2,4,128,4,128]{2,4,3,1,0:T(8,128)(2,1)}, bf16[2,4,128,4,128]{4,3,2,1,0:T(4,128)(2,1)}, f32[2,4,8,128,128]{4,3,2,1,0:T(8,128)},...) while((s32[]{:T(128)}, ...), condition=%wide.region_4.5_spmd, body=%wide.region_0.4_spmd.sunk | while | flops 3275222016 | bytes 217678256 | solution.py:62
  142.4 6.5 %bitcast_dynamic-update-slice_fusion.6 = (bf16[2,4,128,4,128]{2,4,3,1,0:T(8,128)(2,1)}, bf16[4,128,4,128]{3,1,2,0:T(8,128)(2,1)S(1)}) fusion(bf16[2,4,128,4,128]{2,4,3,1,0:T(8,128)(2,1)} %get-tuple-element.241, s32[]{:T(128)} %get-tuple-element.240, bf16[4,8,128,128,1]{3,2,4,1,0:T(8,128)(2,1)S(1)} %bitcast.212, f32[4,4,128]{2,1,0:T(4,128)S(1)} %fusion.102, ...), kind=kOutput, calls=%fused_computation.27.clone.1 | convolution fusion | flops 547618816 | bytes 10502688 | tf_op jit(solution)/shard_map/while/body/eval_jaxpr/nhqkc,nkcd->nqhd/dot_general | solution.py:27
  150.2 4.3 %fusion.103 = bf16[4,4,128,8,128]{2,4,1,3,0:T(8,128)(2,1)S(1)} fusion(f32[4,4,128]{2,1,0:T(4,128)S(1)} %bitcast.225, bf16[4,8,128,128,1]{3,2,4,1,0:T(8,128)(2,1)S(1)} %bitcast.213, bf16[2,4,128,4,128]{2,4,3,1,0:T(8,128)(2,1)} %copy-done.4, s32[]{:T(128)} %get-tuple-element.240, f32[4,4,128]{2,1,0:T(4,128)S(1)} %fusion.102, ...), kind=kOutput, calls=%fused_computation.5.clone.1 | convolution fusion | flops 553648128 | bytes 14180896 | tf_op jit(solution)/shard_map/while/body/eval_jaxpr/nqhd,nkcd->nhqkc/dot_general | solution.py:33
  170.2 6.5 %bitcast_dynamic-update-slice_fusion.6 = (bf16[2,4,128,4,128]{2,4,3,1,0:T(8,128)(2,1)}, bf16[4,128,4,128]{3,1,2,0:T(8,128)(2,1)S(1)}) fusion(bf16[2,4,128,4,128]{2,4,3,1,0:T(8,128)(2,1)} %get-tuple-element.241, s32[]{:T(128)} %get-tuple-element.240, bf16[4,8,128,128,1]{3,2,4,1,0:T(8,128)(2,1)S(1)} %bitcast.212, f32[4,4,128]{2,1,0:T(4,128)S(1)} %fusion.102, ...), kind=kOutput, calls=%fused_computation.27.clone.1 | convolution fusion | flops 547618816 | bytes 10502688 | tf_op jit(solution)/shard_map/while/body/eval_jaxpr/nhqkc,nkcd->nqhd/dot_general | solution.py:27
  178.0 4.3 %fusion.103 = bf16[4,4,128,8,128]{2,4,1,3,0:T(8,128)(2,1)S(1)} fusion(f32[4,4,128]{2,1,0:T(4,128)S(1)} %bitcast.225, bf16[4,8,128,128,1]{3,2,4,1,0:T(8,128)(2,1)S(1)} %bitcast.213, bf16[2,4,128,4,128]{2,4,3,1,0:T(8,128)(2,1)} %copy-done.4, s32[]{:T(128)} %get-tuple-element.240, f32[4,4,128]{2,1,0:T(4,128)S(1)} %fusion.102, ...), kind=kOutput, calls=%fused_computation.5.clone.1 | convolution fusion | flops 553648128 | bytes 14180896 | tf_op jit(solution)/shard_map/while/body/eval_jaxpr/nqhd,nkcd->nhqkc/dot_general | solution.py:33
  187.8 7.2 %fusion.41 = f32[8,128,128]{2,0,1:T(8,128)S(1)} fusion(f32[8,8,128,128]{3,2,1,0:T(8,128)} %bitcast.219, s32[8,8]{0,1:T(8,128)S(1)} %copy-done.14, pred[8,8]{0,1:T(8,128)(4,1)S(1)} %copy-done.15), kind=kOutput, calls=%fused_computation.54 | convolution fusion | flops 100664320 | bytes 4718912 | tf_op jit(solution)/shard_map/bnk,nkcd->bcd/dot_general | solution.py:71
  195.2 5.0 %fusion.44 = f32[8,128,128]{2,0,1:T(8,128)S(1)} fusion(f32[8,8,128,128]{3,2,1,0:T(8,128)S(1)} %bitcast.220, s32[8,8]{0,1:T(8,128)S(1)} %copy-done.14, pred[8,8]{0,1:T(8,128)(4,1)S(1)} %copy-done.15), kind=kOutput, calls=%fused_computation.55 | convolution fusion | flops 100664320 | bytes 4718912 | tf_op jit(solution)/shard_map/bnk,nkcd->bcd/dot_general | solution.py:72
  201.0 10.3 %fusion.47 = f32[4096,512]{0,1:T(8,128)} fusion(bf16[1024,4096]{1,0:T(8,128)(2,1)} %constant_dynamic-update-slice_fusion.1, bf16[128,8,4,128]{3,2,1,0:T(4,128)(2,1)S(1)} %bitcast.227), kind=kOutput, calls=%fused_computation.56 | convolution fusion | flops 4294967296 | bytes 17825792 | tf_op jit(solution)/shard_map/dot_general | solution.py:142
  211.3 4.7 %fusion.53 = f32[4096,128]{0,1:T(8,128)S(1)} fusion(bf16[1024,4096]{1,0:T(8,128)(2,1)} %constant_dynamic-update-slice_fusion.1, s32[]{:T(128)S(6)} %select_n.118, f32[1024,128]{1,0:T(8,128)S(1)} %bitcast.216, f32[1024,128]{1,0:T(8,128)S(1)} %bitcast.218, f32[1024,256]{1,0:T(8,128)S(1)} %collective-permute-done.8), kind=kOutput, calls=%fused_computation.62 | convolution fusion | flops 1074135040 | bytes 12058628 | tf_op jit(solution)/shard_map/dot_general | solution.py:143
  216.0 8.6 %pad_maximum_fusion = f32[4096,640]{0,1:T(8,128)} fusion(f32[4096,128]{0,1:T(8,128)S(1)} %fusion.53, f32[4096,512]{0,1:T(8,128)} %fusion.47), kind=kLoop, calls=%fused_computation.39 | loop fusion | flops 2621440 | bytes 20971520 | tf_op jit(solution)/shard_map/concatenate | solution.py:145
  226.4 18.6 %all_to_all.32 = bf16[8,128,512]{2,1,0:T(8,128)(2,1)S(1)} all-to-all(bf16[8,128,512]{2,1,0:T(8,128)(2,1)S(1)} %copy.102), channel_id=1, replica_groups=mesh['ctx'=8,'dp'=4] {'ctx'}, dimensions={0} | all-to-all | bytes 2097152 | tf_op jit(solution)/shard_map/all_to_all | solution.py:134
  247.0 154.0 %reduce-scatter.2.cloned.1.call-done = f32[1024,640]{0,1:T(8,128)} async-done(((f32[4096,640]{0,1:T(8,128)}), f32[1024,640]{0,1:T(8,128)}) %reduce-scatter.2.cloned.1.call-update) | async-done | bytes 2621456 | tf_op jit(solution)/shard_map/reduce_scatter | solution.py:144
  (134 shorter events, 65.9 us)
Async XLA Ops:
  7.2 13.6 %copy-start = (s32[4,8,8]{2,1,0:T(8,128)S(1)}, s32[4,8,8]{2,1,0:T(8,128)}, u32[]{:S(2)}) copy-start(s32[4,8,8]{2,1,0:T(8,128)} %param.12) | copy-start | bytes 3076
  7.2 32.4 %copy-start.12 = (bf16[1,128,4096]{2,1,0:T(8,128)(2,1)S(1)}, bf16[1,128,4096]{2,1,0:T(8,128)(2,1)}, u32[]{:S(2)}) copy-start(bf16[1,128,4096]{2,1,0:T(8,128)(2,1)} %param.8) | copy-start | bytes 3145732
  7.2 103.8 %all-gather.2.cloned.1.call-start = ((), (), s32[]{:S(2)}) async-start(), calls=%async_computation.3 | async-start | bytes 6553600 | tf_op jit(solution)/shard_map/all_gather | solution.py:89
  9.8 24.8 %collective-permute-start = (bf16[128,4096]{1,0:T(8,128)(2,1)}, bf16[128,4096]{1,0:T(8,128)(2,1)}, u32[]{:S(2)}, u32[]{:S(2)}) collective-permute-start(bf16[128,4096]{1,0:T(8,128)(2,1)} %bitcast.222), channel_id=1, source_target_pairs={{0,4},{4,8},{8,12},{12,16},{16,20},{20,24},{24,28},{28,0},{1,5},{5... | collective-permute-start | bytes 3145736 | tf_op jit(solution)/shard_map/ppermute | solution.py:103
  10.3 30.4 %collective-permute-start.1 = (bf16[128,4096]{1,0:T(8,128)(2,1)}, bf16[128,4096]{1,0:T(8,128)(2,1)S(1)}, u32[]{:S(2)}, u32[]{:S(2)}) collective-permute-start(bf16[128,4096]{1,0:T(8,128)(2,1)} %bitcast.223), channel_id=1, source_target_pairs={{0,28},{4,0},{8,4},{12,8},{16,12},{20,16},{24,20},{28,24},{1,29},{... | collective-permute-start | bytes 3145736 | tf_op jit(solution)/shard_map/ppermute | solution.py:109
  15.6 116.4 %all-to-all-start = ((bf16[128,8,512]{0,2,1:T(8,128)(2,1)}), bf16[128,8,512]{0,2,1:T(8,128)(2,1)S(1)}, u32[]{:S(2)}, u32[]{:S(2)}) async-start(bf16[128,8,512]{0,2,1:T(8,128)(2,1)} %bitcast.38), calls=%async_computation | async-start | bytes 2097152 | tf_op jit(solution)/shard_map/all_to_all | solution.py:129
  19.1 381.9 %reduce-scatter.2.cloned.1.call-start = ((), (), s32[]{:S(2)}) async-start(), calls=%async_computation.4 | async-start | bytes 13107200 | tf_op jit(solution)/shard_map/reduce_scatter | solution.py:144
  34.6 33.6 %collective-permute-start.2 = (bf16[128,4096]{1,0:T(8,128)(2,1)}, bf16[128,4096]{1,0:T(8,128)(2,1)S(1)}, u32[]{:S(2)}, u32[]{:S(2)}) collective-permute-start(bf16[128,4096]{1,0:T(8,128)(2,1)} %collective-permute-done), channel_id=1, source_target_pairs={{0,4},{4,8},{8,12},{12,16},{16,20},{20,24},{24,28},{28,0},{1,5},{5... | collective-permute-start | bytes 3145736 | tf_op jit(solution)/shard_map/ppermute | solution.py:103
  40.7 31.6 %collective-permute-start.3 = (bf16[128,4096]{1,0:T(8,128)(2,1)S(1)}, bf16[128,4096]{1,0:T(8,128)(2,1)S(1)}, u32[]{:S(2)}, u32[]{:S(2)}) collective-permute-start(bf16[128,4096]{1,0:T(8,128)(2,1)S(1)} %collective-permute-done.1), channel_id=1, source_target_pairs={{0,28},{4,0},{8,4},{12,8},{16,12},{20,16},{24,20},{28,24},{1,29},{... | collective-permute-start | bytes 3145736 | tf_op jit(solution)/shard_map/ppermute | solution.py:109
  68.2 20.4 %collective-permute-start.4 = (bf16[128,4096]{1,0:T(8,128)(2,1)S(1)}, bf16[128,4096]{1,0:T(8,128)(2,1)}, u32[]{:S(2)}, u32[]{:S(2)}) collective-permute-start(bf16[128,4096]{1,0:T(8,128)(2,1)S(1)} %collective-permute-done.2), channel_id=1, source_target_pairs={{0,4},{4,8},{8,12},{12,16},{16,20},{20,24},{24,28},{28,0},{1,5},{5... | collective-permute-start | bytes 3145736 | tf_op jit(solution)/shard_map/ppermute | solution.py:103
  72.3 42.5 %collective-permute-start.5 = (bf16[128,4096]{1,0:T(8,128)(2,1)S(1)}, bf16[128,4096]{1,0:T(8,128)(2,1)S(1)}, u32[]{:S(2)}, u32[]{:S(2)}) collective-permute-start(bf16[128,4096]{1,0:T(8,128)(2,1)S(1)} %collective-permute-done.3), channel_id=1, source_target_pairs={{0,28},{4,0},{8,4},{12,8},{16,12},{20,16},{24,20},{28,24},{1,29},{... | collective-permute-start | bytes 3145736 | tf_op jit(solution)/shard_map/ppermute | solution.py:109
  88.6 27.2 %collective-permute-start.6 = (bf16[128,4096]{1,0:T(8,128)(2,1)}, bf16[128,4096]{1,0:T(8,128)(2,1)}, u32[]{:S(2)}, u32[]{:S(2)}) collective-permute-start(bf16[128,4096]{1,0:T(8,128)(2,1)} %collective-permute-done.4), channel_id=1, source_target_pairs={{0,4},{4,8},{8,12},{12,16},{16,20},{20,24},{24,28},{28,0},{1,5},{5... | collective-permute-start | bytes 3145736 | tf_op jit(solution)/shard_map/ppermute | solution.py:103
  112.3 6.4 %collective-permute-start.7 = (bf16[4096,128]{1,0:T(8,128)(2,1)S(1)}, bf16[4096,128]{1,0:T(8,128)(2,1)S(1)}, u32[]{:S(2)}, u32[]{:S(2)}) collective-permute-start(bf16[4096,128]{1,0:T(8,128)(2,1)S(1)} %slice.36), channel_id=1, source_target_pairs={{0,4},{4,0},{8,12},{12,8},{16,20},{20,16},{24,28},{28,24},{1,5},{5... | collective-permute-start | bytes 3145736 | tf_op jit(solution)/shard_map/ppermute | solution.py:14
  131.9 55.8 %copy-start.14 = (s32[8,8]{0,1:T(8,128)S(1)}, s32[8,8]{0,1:T(8,128)}, u32[]{:S(2)}) copy-start(s32[8,8]{0,1:T(8,128)} %copy.68) | copy-start | bytes 772
  132.0 55.8 %copy-start.15 = (pred[8,8]{0,1:T(8,128)(4,1)S(1)}, pred[8,8]{0,1:T(8,128)(4,1)}, u32[]{:S(2)}) copy-start(pred[8,8]{0,1:T(8,128)(4,1)} %iota_compare_fusion.1) | copy-start | bytes 196
  132.2 5.3 %copy-start.4 = (bf16[2,4,128,4,128]{2,4,3,1,0:T(8,128)(2,1)}, bf16[2,4,128,4,128]{2,4,3,1,0:T(8,128)(2,1)S(1)}, u32[]{:S(2)}) copy-start(bf16[2,4,128,4,128]{2,4,3,1,0:T(8,128)(2,1)S(1)} %get-tuple-element.262) | copy-start | bytes 3145732 | tf_op jit(solution)/shard_map/while
  142.4 7.8 %copy-start.3 = (f32[4,8,128,128,4]{3,2,4,1,0:T(8,128)S(1)}, f32[4,8,128,128,4]{3,2,4,1,0:T(8,128)}, u32[]{:S(2)}) copy-start(f32[4,8,128,128,4]{3,2,4,1,0:T(8,128)} %copy-done.2) | copy-start | bytes 25165828 | tf_op jit(solution)/shard_map/while
  154.6 5.4 %copy-start.5 = (bf16[2,4,128,4,128]{2,4,3,1,0:T(8,128)(2,1)S(1)}, bf16[2,4,128,4,128]{2,4,3,1,0:T(8,128)(2,1)}, u32[]{:S(2)}) copy-start(bf16[2,4,128,4,128]{2,4,3,1,0:T(8,128)(2,1)} %copy-done.4) | copy-start | bytes 3145732 | tf_op jit(solution)/shard_map/while
  170.2 7.8 %copy-start.3 = (f32[4,8,128,128,4]{3,2,4,1,0:T(8,128)S(1)}, f32[4,8,128,128,4]{3,2,4,1,0:T(8,128)}, u32[]{:S(2)}) copy-start(f32[4,8,128,128,4]{3,2,4,1,0:T(8,128)} %copy-done.2) | copy-start | bytes 25165828 | tf_op jit(solution)/shard_map/while
  182.3 5.4 %copy-start.5 = (bf16[2,4,128,4,128]{2,4,3,1,0:T(8,128)(2,1)S(1)}, bf16[2,4,128,4,128]{2,4,3,1,0:T(8,128)(2,1)}, u32[]{:S(2)}) copy-start(bf16[2,4,128,4,128]{2,4,3,1,0:T(8,128)(2,1)} %copy-done.4) | copy-start | bytes 3145732 | tf_op jit(solution)/shard_map/while
  187.8 7.4 %copy-start.10 = (f32[2,4,8,128,128]{4,3,2,1,0:T(8,128)S(1)}, f32[2,4,8,128,128]{4,3,2,1,0:T(8,128)}, u32[]{:S(2)}) copy-start(f32[2,4,8,128,128]{4,3,2,1,0:T(8,128)} %get-tuple-element.66) | copy-start | bytes 12582916
  187.8 13.2 %copy-start.16 = (bf16[2,4,128,4,128]{4,3,2,1,0:T(4,128)(2,1)S(1)}, bf16[2,4,128,4,128]{4,3,2,1,0:T(4,128)(2,1)}, u32[]{:S(2)}) copy-start(bf16[2,4,128,4,128]{4,3,2,1,0:T(4,128)(2,1)} %get-tuple-element.64) | copy-start | bytes 3145732
  200.3 10.9 %collective-permute-start.8 = (f32[1024,256]{1,0:T(8,128)S(1)}, f32[1024,256]{1,0:T(8,128)S(1)}, u32[]{:S(2)}, u32[]{:S(2)}) collective-permute-start(f32[1024,256]{1,0:T(8,128)S(1)} %pad_maximum_fusion.2), channel_id=1, source_target_pairs={{0,4},{4,0},{8,12},{12,8},{16,20},{20,16},{24,28},{28,24},{1,5},{5... | collective-permute-start | bytes 3145736 | tf_op jit(solution)/shard_map/ppermute | solution.py:14
  225.9 179.7 %copy-start.1 = (s32[4,8,8]{2,1,0:T(8,128)S(1)}, s32[4,8,8]{2,1,0:T(8,128)}, u32[]{:S(2)}) copy-start(s32[4,8,8]{2,1,0:T(8,128)} %param.12) | copy-start | bytes 3076
  (15 other events, 47.1 us)
Sparse Core Ops, SparseCore 0:
  10.2 100.7 all-gather.1
  224.8 176.1 reduce-scatter.1
